TPU v7x, 512 devices: a whole 4x8x8 slice. The times are simulated.
512 devices in a mesh: cfg: 2 (over y_hi), req: 8 (over y_lo, core), seq: 32 (over z, x).
Axes of the slice: x: 4, y: 8 (y_hi: 2, y_lo: 4; y = y_hi * 4 + y_lo), z: 8, core: 2. Of those that a mesh axis runs over, the one named last changes fastest.
Arguments:
- query: bfloat16 [2, 8, 1024, 768], P('cfg', 'req', 'seq'), may hold values from -6 to 6
- key_value: bfloat16 [2, 2, 8, 1280, 768], P(None, 'cfg', 'req', 'seq'), may hold values from -6 to 6
- residual_in: bfloat16 [2, 8, 1024, 1536], P('cfg', 'req', 'seq'), may hold values from -0.119628906 to 0.119628906
- text_len: int32 [2, 8], P('cfg', 'req'), may hold values from 1 to 154, as said below
- attn_gate: float32 [2, 8, 1536], P('cfg', 'req'), may hold values from 0.5 to 2
- mlp_shift: float32 [2, 8, 1536], P('cfg', 'req'), may hold values from -3 to 3
- mlp_scale: float32 [2, 8, 1536], P('cfg', 'req'), may hold values from -3 to 3
- mlp_gate: float32 [2, 8, 1536], P('cfg', 'req'), may hold values from 0.5 to 2
- shift: float32 [2, 8, 1536], P('cfg', 'req'), may hold values from -3 to 3
- scale: float32 [2, 8, 1536], P('cfg', 'req'), may hold values from -3 to 3
- w_proj: bfloat16 [768, 1536], P(None, 'req'), may hold values from -0.21875 to 0.21875
- w_up: bfloat16 [1536, 3072], P(None, 'req'), may hold values from -0.15625 to 0.15625
- w_down: bfloat16 [3072, 1536], P('req'), may hold values from -0.109375 to 0.109375
- w_out: bfloat16 [1536, 64], replicated, may hold values from -1 to 1
- latent: float32 [8, 1024, 64], P('req', 'seq', 'cfg'), may hold values from -6 to 6
- step_size: float32 [8], P('req'), may hold values from 0.1 to 0.5
Outputs:
- latent_next: float32 [8, 1024, 64], P('req', 'seq', 'cfg')
- guided_norm: float32 [8], P('req')
- peak: float32 [8], P('req')
Inputs may be any that keep to these rules, and one draw needn't show every extreme that they name: `text_len`: some entry equals 154.
All inputs are finite; a program needn't handle non-finite values.
Results may differ from a plain program's by a relative error of at most 0.015.
Values may be sent and summed in bfloat16 or wider, within the bound.
No kernel may reach another device: no remote copies, remote signals or barrier semaphores. Data moves between devices by JAX's collectives and lax.ppermute only.
A program may use at most 64 MiB of HBM per device.

v0:
```python
import jax
import jax.numpy as jnp
from jax import lax
from jax.sharding import PartitionSpec as P

HEADS = 12
HD = 64
guidance_weight = 4.0


def swapped(block, axis, apart):
    count = lax.axis_size(axis)
    route = []
    for low in range(count):
        high = low | 1 << apart
        if high != low and high < count:
            route += [(low, high), (high, low)]
    return lax.ppermute(block, axis, route)


def modulate_rows(hidden, shift_row, scale_row):
    row_mean = jnp.mean(hidden, axis=1, keepdims=True)
    centered = hidden - row_mean
    row_var = jnp.mean(centered * centered, axis=1, keepdims=True)
    return (
        centered * lax.rsqrt(row_var + 1e-06) * (1.0 + scale_row[None, :]) + shift_row[None, :]
    ).astype(jnp.bfloat16)


def per_device(
    query,
    key_value,
    residual_in,
    text_len,
    attn_gate,
    mlp_shift,
    mlp_scale,
    mlp_gate,
    shift,
    scale,
    w_proj,
    w_up,
    w_down,
    w_out,
    latent,
    step_size,
):
    img_dev = query.shape[2]
    rows_dev = key_value.shape[3]
    txt_dev = rows_dev - img_dev
    length = text_len[0, 0]
    queries = query[0, 0].reshape(img_dev, HEADS, HD)
    key_vals = key_value[:, 0, 0]
    factor = HD ** (-0.5)
    piece = lax.all_gather(key_vals, "seq", axis=1, tiled=True)
    running_max = jnp.full((img_dev, HEADS), -1e30, jnp.float32)
    piece_rows = piece.shape[1]
    positions = jnp.arange(piece_rows, dtype=jnp.int32)
    within = positions % rows_dev
    text_slot = positions // rows_dev * txt_dev + within - img_dev
    usable = ((within < img_dev) | (text_slot < length))[None, None, :]
    keys_here = piece[0].reshape(piece_rows, HEADS, HD)
    vals_here = piece[1].reshape(piece_rows, HEADS, HD)
    logits = (
        jnp.einsum("qhd,khd->qhk", queries, keys_here, preferred_element_type=jnp.float32) * factor
    )
    new_max = jnp.maximum(running_max, jnp.max(jnp.where(usable, logits, -1e30), axis=2))
    weights = jnp.where(usable, jnp.exp(logits - new_max[:, :, None]), 0.0)
    running_sum = jnp.sum(weights, axis=2)
    weighted = jnp.einsum(
        "qhk,khd->qhd", weights.astype(jnp.bfloat16), vals_here, preferred_element_type=jnp.float32
    )
    attended = (
        (weighted / running_sum[:, :, None]).reshape(img_dev, HEADS * HD).astype(jnp.bfloat16)
    )
    projected = jnp.dot(
        attended,
        lax.all_gather(w_proj, "req", axis=1, tiled=True),
        preferred_element_type=jnp.float32,
    )
    hidden = residual_in[0, 0].astype(jnp.float32) + attn_gate[0, 0][None, :] * projected
    mlp_in = modulate_rows(hidden, mlp_shift[0, 0], mlp_scale[0, 0])
    inner = jax.nn.gelu(
        jnp.dot(
            lax.all_gather(mlp_in, "req", axis=0, tiled=True),
            w_up,
            preferred_element_type=jnp.float32,
        ),
        approximate=True,
    ).astype(jnp.bfloat16)
    mlp_out = lax.psum_scatter(
        jnp.dot(inner, w_down, preferred_element_type=jnp.float32).astype(jnp.bfloat16),
        "req",
        scatter_dimension=0,
        tiled=True,
    ).astype(jnp.float32)
    hidden_two = hidden + mlp_gate[0, 0][None, :] * mlp_out
    modulated = modulate_rows(hidden_two, shift[0, 0], scale[0, 0])
    velocity = jnp.dot(modulated, w_out, preferred_element_type=jnp.float32)
    half_width = velocity.shape[1] // lax.axis_size("cfg")
    side_index = lax.axis_index("cfg")
    received = swapped(velocity, "cfg", 0)
    is_cond = side_index == 0
    cond_part = jnp.where(is_cond, velocity, received)
    uncond = jnp.where(is_cond, received, velocity)
    guided_full = uncond + guidance_weight * (cond_part - uncond)
    partials = jnp.stack([jnp.sum(guided_full * guided_full), jnp.max(jnp.abs(guided_full))])
    n_seq = lax.axis_size("seq")
    gathered = lax.all_to_all(jnp.broadcast_to(partials[None], (n_seq, 2)), "seq", 0, 0, tiled=True)
    guided_total = jnp.sum(gathered[:, 0])
    peak_value = jnp.max(gathered[:, 1])
    entries = img_dev * n_seq * velocity.shape[1]
    guided_norm = jnp.sqrt(guided_total / entries + 1e-06)
    guided = lax.dynamic_slice_in_dim(guided_full, side_index * half_width, half_width, 1)
    latent_next = latent + step_size[0] * guided[None, :, :]
    return (latent_next, jnp.reshape(guided_norm, (1,)), jnp.reshape(peak_value, (1,)))


def solution(mesh):
    in_specs = (
        P("cfg", "req", "seq", None),
        P(None, "cfg", "req", "seq", None),
        P("cfg", "req", "seq", None),
        P("cfg", "req"),
        P("cfg", "req", None),
        P("cfg", "req", None),
        P("cfg", "req", None),
        P("cfg", "req", None),
        P("cfg", "req", None),
        P("cfg", "req", None),
        P(None, "req"),
        P(None, "req"),
        P("req", None),
        P(),
        P("req", "seq", "cfg"),
        P("req"),
    )
    out_specs = (P("req", "seq", "cfg"), P("req"), P("req"))
    return jax.shard_map(
        per_device, mesh=mesh, in_specs=in_specs, out_specs=out_specs, check_vma=False
    )
```

profile of v0, /device:TPU:2, one launch (start us, length us, event | category | flops | bytes accessed | tf_op | source)
XLA Modules:
  0.0 248.8 jit_solution(4121349338983233270)
XLA Ops:
  7.2 0.0 copy-start
  7.2 0.0 all-gather.6.cloned.1.call-start
  7.2 0.7 all-gather.6.cloned.1.call-update
  7.9 0.0 all-gather.4.cloned.1.call-start
  8.0 0.7 all-gather.4.cloned.1.call-update
  8.7 0.0 reduce-scatter.2.cloned.1.call-start
  9.4 0.9 reshape_squeeze.10
  10.3 0.7 reduce.2
  11.0 0.7 reduce.5
  11.8 0.7 add_reduce_fusion.1
  12.5 89.9 %all-gather.6.cloned.1.call-done = bf16[2,1,1,1280,768]{4,3,2,1,0:T(8,128)(2,1)} async-done(((bf16[2,1,1,40,768]{4,3,2,1,0:T(8,128)(2,1)}), bf16[2,1,1,1280,768]{4,3,2,1,0:T(8,128)(2,1)}) %all-gather.6.cloned.1.call-update) | async-done | bytes 3932176 | tf_op jit(solution)/shard_map/all_gather | solution.py:55
  102.4 4.3 %fusion.46 = (bf16[1,1,1,1280,768]{4,3,2,1,0:T(8,128)(2,1)}, bf16[1,1,1,1280,768]{4,3,2,1,0:T(8,128)(2,1)}) fusion(bf16[2,1,1,1280,768]{4,3,2,1,0:T(8,128)(2,1)} %all-gather.6.cloned.1.call-done), kind=kLoop, calls=%fused_computation.75 | loop fusion | bytes 7864320 | tf_op jit(solution)/shard_map/slice | solution.py:62
  106.7 2.7 %copy.26 = bf16[1,1,1,1280,768]{3,4,2,1,0:T(8,128)(2,1)S(1)} copy(bf16[1,1,1,1280,768]{4,3,2,1,0:T(8,128)(2,1)} %get-tuple-element.8) | data formatting | bytes 3932160 | tf_op jit(solution)/shard_map/slice | solution.py:62
  109.4 4.0 %copy.28 = bf16[1,1,1,1280,768]{3,4,2,1,0:T(8,128)(2,1)} copy(bf16[1,1,1,1280,768]{4,3,2,1,0:T(8,128)(2,1)} %get-tuple-element.9) | data formatting | bytes 3932160 | tf_op jit(solution)/shard_map/slice | solution.py:63
  113.4 0.5 select_reduce_fusion
  113.9 0.0 copy-start.1
  113.9 0.5 fusion.2
  114.4 1.1 copy-done.1
  115.5 0.0 copy-start.3
  115.5 0.7 fusion.5
  116.3 0.1 convert_element_type.34
  116.4 27.9 %all-gather.4.cloned.1.call-done = bf16[768,1536]{0,1:T(8,128)(2,1)} async-done(((bf16[768,192]{0,1:T(8,128)(2,1)}), bf16[768,1536]{0,1:T(8,128)(2,1)}) %all-gather.4.cloned.1.call-update) | async-done | bytes 2359312 | tf_op jit(solution)/shard_map/all_gather | solution.py:78
  144.3 0.0 copy-done.3
  144.3 2.6 %fusion.47 = (f32[32]{0:T(128)S(1)}, f32[32,1536]{1,0:T(8,128)S(1)}) fusion(bf16[32,768]{1,0:T(8,128)(2,1)S(1)} %convert_element_type.34, bf16[768,1536]{0,1:T(8,128)(2,1)} %all-gather.4.cloned.1.call-done, f32[1536]{0:T(1024)S(1)} %reduce.2, bf16[1,1,32,1536]{3,2,1,0:T(8,128)(2,1)S(1)} %copy-done.3), kind=kOutput, calls=%fused_computation.76 | convolution fusion | flops 75694048 | bytes 2709632 | tf_op jit(solution)/shard_map/dot_general | solution.py:76
  146.9 0.2 multiply_reduce_fusion.1
  147.1 0.1 add_convert_fusion.1
  147.2 15.2 %all_gather.11 = bf16[256,1536]{1,0:T(8,128)(2,1)S(1)} all-gather(bf16[32,1536]{1,0:T(8,128)(2,1)S(1)} %add_convert_fusion.1), channel_id=1, replica_groups=mesh['cfg'=2,'req'=8,'seq'=32] {'req'}, dimensions={0}, use_global_device_ids=true | all-gather | bytes 884736 | tf_op jit(solution)/shard_map/all_gather | solution.py:85
  162.4 0.0 copy-done
  162.4 0.0 copy-start.6
  162.4 0.0 copy-start.7
  162.4 0.0 copy-start.5
  162.4 0.0 copy-start.2
  162.4 3.3 %convolution_convert_fusion = bf16[256,1536]{1,0:T(8,128)(2,1)} fusion(bf16[384,1536]{1,0:T(8,128)(2,1)S(1)} %copy-done, bf16[256,1536]{1,0:T(8,128)(2,1)S(1)} %all_gather.11, bf16[1536,384]{1,0:T(8,128)(2,1)} %param.27), kind=kOutput, calls=%fused_computation.2 | convolution fusion | flops 605257728 | bytes 3932160 | tf_op jit(solution)/shard_map/dot_general | solution.py:92
  165.8 0.0 copy-start.4
  165.8 0.0 reduce-scatter.2.cloned.1.call-update
  165.8 0.0 copy-done.6
  165.8 0.0 copy-done.7
  165.9 0.0 copy-done.5
  165.9 39.4 %reduce-scatter.2.cloned.1.call-done = bf16[32,1536]{1,0:T(8,128)(2,1)} async-done(((bf16[256,1536]{1,0:T(8,128)(2,1)}), bf16[32,1536]{1,0:T(8,128)(2,1)}) %reduce-scatter.2.cloned.1.call-update) | async-done | bytes 98320 | tf_op jit(solution)/shard_map/reduce_scatter | solution.py:91
  205.3 1.0 fusion.29
  206.3 1.1 multiply_reduce_fusion
  207.4 0.0 copy-done.2
  207.4 1.1 fusion.23
  208.6 4.8 %collective-permute-start = (f32[32,64]{1,0:T(8,128)S(1)}, f32[32,64]{1,0:T(8,128)S(1)}, u32[]{:S(2)}, u32[]{:S(2)}) collective-permute-start(f32[32,64]{1,0:T(8,128)S(1)} %fusion.23), channel_id=1, source_target_pairs={{0,256},{256,0},{1,257},{257,1},{2,258},{258,2},{3,259},{259,3},{4... | collective-permute-start | bytes 24584 | tf_op jit(solution)/shard_map/ppermute | solution.py:18
  214.0 4.1 %collective-permute-done = f32[32,64]{1,0:T(8,128)S(1)} collective-permute-done((f32[32,64]{1,0:T(8,128)S(1)}, f32[32,64]{1,0:T(8,128)S(1)}, u32[]{:S(2)}, u32[]{:S(2)}) %collective-permute-start) | collective-permute-done | bytes 8224 | tf_op jit(solution)/shard_map/ppermute | solution.py:18
  218.1 0.6 multiply_reduce_fusion.2
  218.7 1.4 pad_maximum_fusion
  220.1 0.6 broadcast_in_dim.39
  220.7 10.5 %all-to-all-start = ((f32[32,1,2]{2,1,0:T(1,128)}), f32[32,1,2]{2,1,0:T(1,128)S(1)}, u32[]{:S(2)}, u32[]{:S(2)}) async-start(f32[32,1,2]{2,1,0:T(1,128)} %broadcast_in_dim.39), calls=%async_computation.1 | async-start | bytes 32768 | tf_op jit(solution)/shard_map/all_to_all | solution.py:109
  231.2 0.0 copy-done.4
  231.2 0.7 bitcast_add_fusion
  231.9 7.8 %all-to-all-done = f32[32,1,2]{2,1,0:T(1,128)S(1)} async-done(((f32[32,1,2]{2,1,0:T(1,128)}), f32[32,1,2]{2,1,0:T(1,128)S(1)}, u32[]{:S(2)}, u32[]{:S(2)}) %all-to-all-start) | async-done | bytes 288 | tf_op jit(solution)/shard_map/all_to_all | solution.py:109
  239.7 0.1 copy.30
  239.8 0.6 slice_reduce_fusion
  (10 shorter events, 0.2 us)
Async XLA Ops:
  7.2 155.3 %copy-start = (bf16[384,1536]{1,0:T(8,128)(2,1)S(1)}, bf16[384,1536]{1,0:T(8,128)(2,1)}, u32[]{:S(2)}) copy-start(bf16[384,1536]{1,0:T(8,128)(2,1)} %param.28) | copy-start | bytes 3538948
  7.2 95.2 %all-gather.6.cloned.1.call-start = ((), (), s32[]{:S(2)}) async-start(), calls=%async_computation.4 | async-start | bytes 4055040 | tf_op jit(solution)/shard_map/all_gather | solution.py:55
  7.9 136.4 %all-gather.4.cloned.1.call-start = ((), (), s32[]{:S(2)}) async-start(), calls=%async_computation.2 | async-start | bytes 2654208 | tf_op jit(solution)/shard_map/all_gather | solution.py:78
  8.7 196.6 %reduce-scatter.2.cloned.1.call-start = ((), (), s32[]{:S(2)}) async-start(), calls=%async_computation.3 | async-start | bytes 884736 | tf_op jit(solution)/shard_map/reduce_scatter | solution.py:91
  113.9 1.6 copy-start.1
  115.5 28.8 %copy-start.3 = (bf16[1,1,32,1536]{3,2,1,0:T(8,128)(2,1)S(1)}, bf16[1,1,32,1536]{3,2,1,0:T(8,128)(2,1)}, u32[]{:S(2)}) copy-start(bf16[1,1,32,1536]{3,2,1,0:T(8,128)(2,1)} %param.18) | copy-start | bytes 294916
  162.4 3.4 %copy-start.6 = (f32[1,1,1536]{2,1,0:T(1,128)S(1)}, f32[1,1,1536]{2,1,0:T(1,128)}, u32[]{:S(2)}) copy-start(f32[1,1,1536]{2,1,0:T(1,128)} %param.23) | copy-start | bytes 18436
  162.4 3.4 %copy-start.7 = (f32[1,1,1536]{2,1,0:T(1,128)S(1)}, f32[1,1,1536]{2,1,0:T(1,128)}, u32[]{:S(2)}) copy-start(f32[1,1,1536]{2,1,0:T(1,128)} %param.24) | copy-start | bytes 18436
  162.4 3.4 %copy-start.5 = (f32[1,1,1536]{2,1,0:T(1,128)S(1)}, f32[1,1,1536]{2,1,0:T(1,128)}, u32[]{:S(2)}) copy-start(f32[1,1,1536]{2,1,0:T(1,128)} %param.25) | copy-start | bytes 18436
  162.4 45.0 %copy-start.2 = (bf16[1536,64]{0,1:T(8,128)(2,1)S(1)}, bf16[1536,64]{0,1:T(8,128)(2,1)}, u32[]{:S(2)}) copy-start(bf16[1536,64]{0,1:T(8,128)(2,1)} %param.29) | copy-start | bytes 589828
  165.8 65.4 %copy-start.4 = (f32[1,32,32]{2,1,0:T(8,128)S(1)}, f32[1,32,32]{2,1,0:T(8,128)}, u32[]{:S(2)}) copy-start(f32[1,32,32]{2,1,0:T(8,128)} %param.30) | copy-start | bytes 12292
  208.6 9.5 %collective-permute-start = (f32[32,64]{1,0:T(8,128)S(1)}, f32[32,64]{1,0:T(8,128)S(1)}, u32[]{:S(2)}, u32[]{:S(2)}) collective-permute-start(f32[32,64]{1,0:T(8,128)S(1)} %fusion.23), channel_id=1, source_target_pairs={{0,256},{256,0},{1,257},{257,1},{2,258},{258,2},{3,259},{259,3},{4... | collective-permute-start | bytes 24584 | tf_op jit(solution)/shard_map/ppermute | solution.py:18
  220.7 19.0 %all-to-all-start = ((f32[32,1,2]{2,1,0:T(1,128)}), f32[32,1,2]{2,1,0:T(1,128)S(1)}, u32[]{:S(2)}, u32[]{:S(2)}) async-start(f32[32,1,2]{2,1,0:T(1,128)} %broadcast_in_dim.39), calls=%async_computation.1 | async-start | bytes 32768 | tf_op jit(solution)/shard_map/all_to_all | solution.py:109
Sparse Core Ops, SparseCore 0:
  11.2 91.1 all-gather.5
  104.5 39.7 all-gather.3
  165.9 39.3 reduce-scatter.1
where the time goes:
time: 249 us
  waiting for transfers between devices  171 us (69%)
  between operations  17 us (7%)
  starting transfers between devices  15.4 us (6%)
  blocking collectives  15.2 us (6%)
  local copies, waits for them, and re-layouts  13.8 us (6%)
  other arithmetic  8.45 us (3%)
  matrix products  8.28 us (3%)
    all_gather x1, waiting for transfers between devices, per_device(): piece = lax.all_gather(key_vals, 'seq', axis=1, tiled=True)  89.9 us
    reduce_scatter x1, waiting for transfers between devices, per_device(): lax.psum_scatter(jnp.dot(inner, w_down, preferred_element_type=jnp.float3...  39.4 us
    all_gather x1, waiting for transfers between devices, per_device(): lax.all_gather(w_proj, 'req', axis=1, tiled=True)  27.9 us
    all_gather x1, blocking collectives, per_device(): lax.all_gather(mlp_in, 'req', axis=0, tiled=True)  15.2 us
    all_to_all x1, starting transfers between devices, per_device(): lax.all_to_all(jnp.broadcast_to(partials[None], (n_seq, 2)), 'seq', 0, 0,...  10.5 us
    all_to_all x1, waiting for transfers between devices, per_device(): lax.all_to_all(jnp.broadcast_to(partials[None], (n_seq, 2)), 'seq', 0, 0,...  7.82 us
    slice x2, local copies, waits for them, and re-layouts, per_device(): keys_here = piece[0].reshape(piece_rows, HEADS, HD)  6.95 us
  transfers between devices with their start and end apart: 5, of which 5 were waited for; matrix products, arithmetic and copies ran while one was open for 7% of the time, Pallas kernels for 0%

commit v1 on v0

--- a/solution.py
+++ b/solution.py
@@ -45,6 +45,13 @@
     latent,
     step_size,
 ):
+
+    def _review_vectors(base_x):
+        net_axis = "seq"
+        wide_out = jnp.concatenate([base_x for _ in range(lax.axis_size(net_axis))], axis=1)
+        new = lax.all_to_all(wide_out, split_axis=1, tiled=True, concat_axis=1, axis_name=net_axis)
+        return new
+
     img_dev = query.shape[2]
     rows_dev = key_value.shape[3]
     txt_dev = rows_dev - img_dev
@@ -52,7 +59,7 @@
     queries = query[0, 0].reshape(img_dev, HEADS, HD)
     key_vals = key_value[:, 0, 0]
     factor = HD ** (-0.5)
-    piece = lax.all_gather(key_vals, "seq", axis=1, tiled=True)
+    piece = _review_vectors(key_vals)
     running_max = jnp.full((img_dev, HEADS), -1e30, jnp.float32)
     piece_rows = piece.shape[1]
     positions = jnp.arange(piece_rows, dtype=jnp.int32)

time: 249 us -> 280 us (1.12)
  local copies, waits for them, and re-layouts: 13.8 us -> 65.2 us
  waiting for transfers between devices: 171 us -> 137 us
  starting transfers between devices: 15.4 us -> 28.9 us
    all_gather x1 -> x0, waiting for transfers between devices: 89.9 us -> none  [per_device(): piece = lax.all_gather(key_vals, 'seq', axis=1, tiled=True)]
    all_to_all x0 -> x1, waiting for transfers between devices: none -> 86.4 us  [_review_vectors(): lax.all_to_all(wide_out, split_axis=1, tiled=True, concat_axis=1, axis_na...]
    unnamed x16 -> x57, local copies, waits for them, and re-layouts: 1.1 us -> 38.2 us
    all_gather x1, waiting for transfers between devices: 27.9 us -> 0.02 us  [per_device(): lax.all_gather(w_proj, 'req', axis=1, tiled=True)]
    all_to_all x0 -> x1, starting transfers between devices: none -> 13.7 us  [_review_vectors(): lax.all_to_all(wide_out, split_axis=1, tiled=True, concat_axis=1, axis_na...]
    slice x2, local copies, waits for them, and re-layouts: 6.95 us -> 16.7 us  [per_device(): keys_here = piece[0].reshape(piece_rows, HEADS, HD)]
    slice x1, local copies, waits for them, and re-layouts: 4.01 us -> 8.63 us  [per_device(): vals_here = piece[1].reshape(piece_rows, HEADS, HD)]
  transfers between devices with their start and end apart: 5 -> 5, of which waited for: 5 -> 4; matrix products, arithmetic and copies ran while one was open for 7% -> 10% of each run, Pallas kernels for 0% -> 0%
where the time goes in v1:
time: 280 us; the launch traced here: 279 us
  waiting for transfers between devices  137 us (49%)
  local copies, waits for them, and re-layouts  65.2 us (23%)
  starting transfers between devices  28.9 us (10%)
  between operations  17.5 us (6%)
  blocking collectives  15.8 us (6%)
  matrix products  8.22 us (3%)
  other arithmetic  6.36 us (2%)
    all_to_all x1, waiting for transfers between devices, _review_vectors(): lax.all_to_all(wide_out, split_axis=1, tiled=True, concat_axis=1, axis_na...  86.4 us
    unnamed x57, local copies, waits for them, and re-layouts  38.2 us
    reduce_scatter x1, waiting for transfers between devices, per_device(): lax.psum_scatter(jnp.dot(inner, w_down, preferred_element_type=jnp.float3...  38.1 us
    slice x2, local copies, waits for them, and re-layouts, per_device(): keys_here = piece[0].reshape(piece_rows, HEADS, HD)  16.7 us
    all_gather x1, blocking collectives, per_device(): lax.all_gather(mlp_in, 'req', axis=0, tiled=True)  15.8 us
    all_to_all x1, starting transfers between devices, _review_vectors(): lax.all_to_all(wide_out, split_axis=1, tiled=True, concat_axis=1, axis_na...  13.7 us
    all_to_all x1, starting transfers between devices, per_device(): lax.all_to_all(jnp.broadcast_to(partials[None], (n_seq, 2)), 'seq', 0, 0,...  10.5 us
    slice x1, local copies, waits for them, and re-layouts, per_device(): vals_here = piece[1].reshape(piece_rows, HEADS, HD)  8.63 us
  transfers between devices with their start and end apart: 5, of which 4 were waited for; matrix products, arithmetic and copies ran while one was open for 10% of the time, Pallas kernels for 0%

profile of v1, /device:TPU:2, one launch (start us, length us, event | category | flops | bytes accessed | tf_op | source)
XLA Modules:
  0.0 279.2 jit_solution(7041771803221905791)
XLA Ops:
  7.2 1.8 bitcast_dynamic-update-slice_fusion.30
  8.9 1.7 bitcast_dynamic-update-slice_fusion.29
  10.6 1.6 bitcast_dynamic-update-slice_fusion.28
  12.2 1.6 bitcast_dynamic-update-slice_fusion.27
  13.9 1.6 bitcast_dynamic-update-slice_fusion.26
  15.5 1.6 bitcast_dynamic-update-slice_fusion.25
  17.2 1.6 bitcast_dynamic-update-slice_fusion.24
  18.8 1.6 bitcast_dynamic-update-slice_fusion.23
  20.4 1.6 bitcast_dynamic-update-slice_fusion.22
  22.1 1.6 bitcast_dynamic-update-slice_fusion.21
  23.7 1.6 bitcast_dynamic-update-slice_fusion.20
  25.4 1.6 bitcast_dynamic-update-slice_fusion.19
  27.0 1.6 bitcast_dynamic-update-slice_fusion.18
  28.7 1.7 bitcast_dynamic-update-slice_fusion.17
  30.3 1.6 bitcast_dynamic-update-slice_fusion.16
  32.0 1.6 bitcast_dynamic-update-slice_fusion.15
  33.6 0.7 bitcast_dynamic-update-slice_fusion.14
  34.4 0.8 bitcast_dynamic-update-slice_fusion.13
  35.1 0.8 bitcast_dynamic-update-slice_fusion.12
  35.9 0.7 bitcast_dynamic-update-slice_fusion.11
  36.6 0.7 bitcast_dynamic-update-slice_fusion.10
  37.4 0.7 bitcast_dynamic-update-slice_fusion.9
  38.1 0.8 bitcast_dynamic-update-slice_fusion.8
  38.9 0.7 bitcast_dynamic-update-slice_fusion.7
  39.6 0.8 bitcast_dynamic-update-slice_fusion.6
  40.3 0.7 bitcast_dynamic-update-slice_fusion.5
  41.1 0.7 bitcast_dynamic-update-slice_fusion.4
  41.8 0.7 bitcast_dynamic-update-slice_fusion.3
  42.6 0.7 bitcast_dynamic-update-slice_fusion.2
  43.3 0.7 bitcast_dynamic-update-slice_fusion.1
  44.0 0.8 bitcast_dynamic-update-slice_fusion
  44.8 0.7 bitcast_dynamic-update-slice_fusion.31
  45.5 13.7 %all-to-all-start = ((bf16[2,1280,768]{2,0,1:T(2,128)(2,1)}), bf16[2,1280,768]{2,0,1:T(2,128)(2,1)}, u32[]{:S(2)}, u32[]{:S(2)}) async-start(bf16[2,1280,768]{2,0,1:T(2,128)(2,1)} %bitcast_dynamic-update-slice_fusion.31), calls=%async_computation | async-start | bytes 7864320 | tf_op jit(solution)/shard_map/all_to_all | solution.py:52
  59.2 0.0 all-gather.2.cloned.1.call-start
  59.3 0.7 all-gather.2.cloned.1.call-update
  60.6 0.1 reshape_squeeze.11
  60.9 86.4 %all-to-all-done = bf16[2,1280,768]{2,0,1:T(2,128)(2,1)} async-done(((bf16[2,1280,768]{2,0,1:T(2,128)(2,1)}), bf16[2,1280,768]{2,0,1:T(2,128)(2,1)}, u32[]{:S(2)}, u32[]{:S(2)}) %all-to-all-start) | async-done | bytes 3932192 | tf_op jit(solution)/shard_map/all_to_all | solution.py:52
  147.4 9.4 %fusion.46 = (bf16[1,1280,768]{2,0,1:T(2,128)(2,1)}, bf16[1,1280,768]{2,0,1:T(2,128)(2,1)}) fusion(bf16[2,1280,768]{2,0,1:T(2,128)(2,1)} %all-to-all-done), kind=kLoop, calls=%fused_computation.107 | loop fusion | bytes 7864320 | tf_op jit(solution)/shard_map/slice | solution.py:69
  156.8 7.2 %copy.28 = bf16[1,1280,768]{1,2,0:T(8,128)(2,1)S(1)} copy(bf16[1,1280,768]{2,0,1:T(2,128)(2,1)} %get-tuple-element.8) | data formatting | bytes 3932160 | tf_op jit(solution)/shard_map/slice | solution.py:69
  164.0 8.6 %copy.27 = bf16[1,1280,768]{1,2,0:T(8,128)(2,1)} copy(bf16[1,1280,768]{2,0,1:T(2,128)(2,1)} %get-tuple-element.9) | data formatting | bytes 3932160 | tf_op jit(solution)/shard_map/slice | solution.py:70
  172.7 0.5 select_reduce_fusion
  173.2 0.5 fusion.2
  173.7 0.5 copy-done.2
  174.2 0.7 fusion.5
  175.0 0.1 convert_element_type.34
  175.1 2.6 fusion.47
  177.8 0.2 multiply_reduce_fusion.1
  178.0 0.1 add_convert_fusion.1
  178.1 15.8 %all_gather.7 = bf16[256,1536]{1,0:T(8,128)(2,1)S(1)} all-gather(bf16[32,1536]{1,0:T(8,128)(2,1)S(1)} %add_convert_fusion.1), channel_id=1, replica_groups=mesh['cfg'=2,'req'=8,'seq'=32] {'req'}, dimensions={0}, use_global_device_ids=true | all-gather | bytes 884736 | tf_op jit(solution)/shard_map/all_gather | solution.py:92
  193.9 3.3 %convolution_convert_fusion = bf16[256,1536]{1,0:T(8,128)(2,1)} fusion(bf16[384,1536]{1,0:T(8,128)(2,1)S(1)} %copy-done, bf16[256,1536]{1,0:T(8,128)(2,1)S(1)} %all_gather.7, bf16[1536,384]{1,0:T(8,128)(2,1)} %param.27), kind=kOutput, calls=%fused_computation.2 | convolution fusion | flops 605257728 | bytes 3932160 | tf_op jit(solution)/shard_map/dot_general | solution.py:99
  197.3 38.1 %reduce-scatter.2.cloned.1.call-done = bf16[32,1536]{1,0:T(8,128)(2,1)} async-done(((bf16[256,1536]{1,0:T(8,128)(2,1)}), bf16[32,1536]{1,0:T(8,128)(2,1)}) %reduce-scatter.2.cloned.1.call-update) | async-done | bytes 98320 | tf_op jit(solution)/shard_map/reduce_scatter | solution.py:98
  235.4 1.0 fusion.29
  236.5 1.1 multiply_reduce_fusion
  237.6 1.1 fusion.23
  238.7 4.6 %collective-permute-start = (f32[32,64]{1,0:T(8,128)S(1)}, f32[32,64]{1,0:T(8,128)S(1)}, u32[]{:S(2)}, u32[]{:S(2)}) collective-permute-start(f32[32,64]{1,0:T(8,128)S(1)} %fusion.23), channel_id=1, source_target_pairs={{0,256},{256,0},{1,257},{257,1},{2,258},{258,2},{3,259},{259,3},{4... | collective-permute-start | bytes 24584 | tf_op jit(solution)/shard_map/ppermute | solution.py:18
  244.0 4.2 %collective-permute-done = f32[32,64]{1,0:T(8,128)S(1)} collective-permute-done((f32[32,64]{1,0:T(8,128)S(1)}, f32[32,64]{1,0:T(8,128)S(1)}, u32[]{:S(2)}, u32[]{:S(2)}) %collective-permute-start) | collective-permute-done | bytes 8224 | tf_op jit(solution)/shard_map/ppermute | solution.py:18
  248.2 0.6 multiply_reduce_fusion.2
  248.8 1.4 pad_maximum_fusion
  250.2 0.6 broadcast_in_dim.39
  250.8 10.5 %all-to-all-start.1 = ((f32[32,1,2]{2,1,0:T(1,128)}), f32[32,1,2]{2,1,0:T(1,128)S(1)}, u32[]{:S(2)}, u32[]{:S(2)}) async-start(f32[32,1,2]{2,1,0:T(1,128)} %broadcast_in_dim.39), calls=%async_computation.2 | async-start | bytes 32768 | tf_op jit(solution)/shard_map/all_to_all | solution.py:116
  261.3 0.7 bitcast_add_fusion
  262.0 7.8 %all-to-all-done.1 = f32[32,1,2]{2,1,0:T(1,128)S(1)} async-done(((f32[32,1,2]{2,1,0:T(1,128)}), f32[32,1,2]{2,1,0:T(1,128)S(1)}, u32[]{:S(2)}, u32[]{:S(2)}) %all-to-all-start.1) | async-done | bytes 288 | tf_op jit(solution)/shard_map/all_to_all | solution.py:116
  269.9 0.1 copy.31
  269.9 0.6 slice_reduce_fusion
  (41 shorter events, 0.4 us)
Async XLA Ops:
  7.2 186.7 %copy-start = (bf16[384,1536]{1,0:T(8,128)(2,1)S(1)}, bf16[384,1536]{1,0:T(8,128)(2,1)}, u32[]{:S(2)}) copy-start(bf16[384,1536]{1,0:T(8,128)(2,1)} %param.28) | copy-start | bytes 3538948
  7.2 26.4 %copy-start.1 = (bf16[2,1,1,40,768]{4,3,2,1,0:T(8,128)(2,1)S(1)}, bf16[2,1,1,40,768]{4,3,2,1,0:T(8,128)(2,1)}, u32[]{:S(2)}) copy-start(bf16[2,1,1,40,768]{4,3,2,1,0:T(8,128)(2,1)} %param.17) | copy-start | bytes 368644
  45.5 15.1 %copy-start.5 = (bf16[1,1,32,768]{3,2,1,0:T(8,128)(2,1)S(1)}, bf16[1,1,32,768]{3,2,1,0:T(8,128)(2,1)}, u32[]{:S(2)}) copy-start(bf16[1,1,32,768]{3,2,1,0:T(8,128)(2,1)} %param.16) | copy-start | bytes 147460
  45.5 15.3 %copy-start.9 = (f32[1,1,1536]{2,1,0:T(1,128)S(1)}, f32[1,1,1536]{2,1,0:T(1,128)}, u32[]{:S(2)}) copy-start(f32[1,1,1536]{2,1,0:T(1,128)} %param.20) | copy-start | bytes 18436
  45.5 15.3 %copy-start.10 = (f32[1,1,1536]{2,1,0:T(1,128)S(1)}, f32[1,1,1536]{2,1,0:T(1,128)}, u32[]{:S(2)}) copy-start(f32[1,1,1536]{2,1,0:T(1,128)} %param.21) | copy-start | bytes 18436
  45.5 15.4 %copy-start.7 = (f32[1,1,1536]{2,1,0:T(1,128)S(1)}, f32[1,1,1536]{2,1,0:T(1,128)}, u32[]{:S(2)}) copy-start(f32[1,1,1536]{2,1,0:T(1,128)} %param.22) | copy-start | bytes 18436
  45.5 101.8 %all-to-all-start = ((bf16[2,1280,768]{2,0,1:T(2,128)(2,1)}), bf16[2,1280,768]{2,0,1:T(2,128)(2,1)}, u32[]{:S(2)}, u32[]{:S(2)}) async-start(bf16[2,1280,768]{2,0,1:T(2,128)(2,1)} %bitcast_dynamic-update-slice_fusion.31), calls=%async_computation | async-start | bytes 7864320 | tf_op jit(solution)/shard_map/all_to_all | solution.py:52
  59.2 115.9 %all-gather.2.cloned.1.call-start = ((), (), s32[]{:S(2)}) async-start(), calls=%async_computation.3 | async-start | bytes 2654208 | tf_op jit(solution)/shard_map/all_gather | solution.py:85
  59.9 175.5 %reduce-scatter.2.cloned.1.call-start = ((), (), s32[]{:S(2)}) async-start(), calls=%async_computation.4 | async-start | bytes 884736 | tf_op jit(solution)/shard_map/reduce_scatter | solution.py:98
  172.7 1.5 copy-start.2
  173.2 1.9 copy-start.4
  177.7 19.5 %copy-start.11 = (f32[1,1,1536]{2,1,0:T(1,128)S(1)}, f32[1,1,1536]{2,1,0:T(1,128)}, u32[]{:S(2)}) copy-start(f32[1,1,1536]{2,1,0:T(1,128)} %param.23) | copy-start | bytes 18436
  177.7 19.5 %copy-start.12 = (f32[1,1,1536]{2,1,0:T(1,128)S(1)}, f32[1,1,1536]{2,1,0:T(1,128)}, u32[]{:S(2)}) copy-start(f32[1,1,1536]{2,1,0:T(1,128)} %param.24) | copy-start | bytes 18436
  177.7 19.5 %copy-start.8 = (f32[1,1,1536]{2,1,0:T(1,128)S(1)}, f32[1,1,1536]{2,1,0:T(1,128)}, u32[]{:S(2)}) copy-start(f32[1,1,1536]{2,1,0:T(1,128)} %param.25) | copy-start | bytes 18436
  177.8 59.8 %copy-start.3 = (bf16[1536,64]{0,1:T(8,128)(2,1)S(1)}, bf16[1536,64]{0,1:T(8,128)(2,1)}, u32[]{:S(2)}) copy-start(bf16[1536,64]{0,1:T(8,128)(2,1)} %param.29) | copy-start | bytes 589828
  178.0 83.4 %copy-start.6 = (f32[1,32,32]{2,1,0:T(8,128)S(1)}, f32[1,32,32]{2,1,0:T(8,128)}, u32[]{:S(2)}) copy-start(f32[1,32,32]{2,1,0:T(8,128)} %param.30) | copy-start | bytes 12292
  238.7 9.5 %collective-permute-start = (f32[32,64]{1,0:T(8,128)S(1)}, f32[32,64]{1,0:T(8,128)S(1)}, u32[]{:S(2)}, u32[]{:S(2)}) collective-permute-start(f32[32,64]{1,0:T(8,128)S(1)} %fusion.23), channel_id=1, source_target_pairs={{0,256},{256,0},{1,257},{257,1},{2,258},{258,2},{3,259},{259,3},{4... | collective-permute-start | bytes 24584 | tf_op jit(solution)/shard_map/ppermute | solution.py:18
  250.8 19.0 %all-to-all-start.1 = ((f32[32,1,2]{2,1,0:T(1,128)}), f32[32,1,2]{2,1,0:T(1,128)S(1)}, u32[]{:S(2)}, u32[]{:S(2)}) async-start(f32[32,1,2]{2,1,0:T(1,128)} %broadcast_in_dim.39), calls=%async_computation.2 | async-start | bytes 32768 | tf_op jit(solution)/shard_map/all_to_all | solution.py:116
Sparse Core Ops, SparseCore 0:
  62.1 43.7 all-gather.1
  197.3 38.0 reduce-scatter.1
